TPU v7x, 512 devices: a whole 4x4x16 slice. The times are simulated.
512 devices in a mesh: grp: 16 (over z), lat: 32 (over y, x, core).
Axes of the slice: x: 4, y: 4, z: 16, core: 2. Of those that a mesh axis runs over, the one named last changes fastest.
Arguments:
- stream: bfloat16 [256, 8192], P('lat'), may hold values from -26 to 26
- batch_index: int32 [256], replicated, may hold values from 0 to 255
- weight: bfloat16 [8192, 65536], P(None, ('grp', 'lat')), may hold values from -0.26516504 to 0.26516504
- enc_bias: float32 [65536], P(('grp', 'lat')), may hold values from -1.5 to 0.5
- dec_bias: float32 [8192], replicated, may hold values from -3 to 3
Outputs:
- weight_grad: bfloat16 [8192, 65536], P(None, ('grp', 'lat'))
- bias_grad: float32 [65536], P(('grp', 'lat'))
- recon_error: bfloat16 [256, 8192], P('lat')
All inputs are finite; a program needn't handle non-finite values.
Results may differ from a plain program's by a relative error of at most 0.025.
Values may be sent and summed in bfloat16 or wider, within the bound.
No kernel may reach another device: no remote copies, remote signals or barrier semaphores. Data moves between devices by JAX's collectives and lax.ppermute only.
A program may use at most 64 MiB of HBM per device.

v0:
```python
import jax
import jax.numpy as jnp
from jax import lax
from jax.sharding import PartitionSpec as P

sharpness = 8.0
penalty = 0.25
epsilon = 1e-06


def body(stream, batch_index, weight, enc_bias, dec_bias):
    own_rows = stream.shape[0]
    rank_lat = lax.axis_index("lat")
    gathered = lax.all_gather(stream, "lat", axis=0, tiled=True)
    batch = jnp.take(gathered, batch_index, axis=0)
    centered = (batch.astype(jnp.float32) - dec_bias).astype(jnp.bfloat16)
    preact = jnp.dot(centered, weight, preferred_element_type=jnp.float32) + enc_bias
    active = (jax.nn.softplus(sharpness * preact) / sharpness).astype(jnp.bfloat16)
    first_row = rank_lat * own_rows
    own_batch = lax.dynamic_slice_in_dim(batch, first_row, own_rows, 0)
    block_recon = lax.psum_scatter(
        lax.dot_general(
            active, weight, (((1,), (1,)), ((), ())), preferred_element_type=jnp.float32
        ).astype(jnp.bfloat16),
        "lat",
        scatter_dimension=0,
        tiled=True,
    )
    recon = lax.psum(block_recon, "grp").astype(jnp.float32)
    error_own = recon + dec_bias - own_batch.astype(jnp.float32)
    grad_own = (2.0 * error_own).astype(jnp.bfloat16)
    grad_rows = lax.all_gather(grad_own, "lat", axis=0, tiled=True)
    grad_active = jnp.dot(grad_rows, weight, preferred_element_type=jnp.float32)
    decoder_grad = lax.dot_general(
        grad_rows, active, (((0,), (0,)), ((), ())), preferred_element_type=jnp.float32
    )
    grad_pre = (grad_active + penalty) * jax.nn.sigmoid(sharpness * preact)
    encoder_grad = lax.dot_general(
        centered,
        grad_pre.astype(jnp.bfloat16),
        (((0,), (0,)), ((), ())),
        preferred_element_type=jnp.float32,
    )
    grad_raw = encoder_grad + decoder_grad
    bias_raw = jnp.sum(grad_pre, axis=0)
    local_squares = jnp.sum(grad_raw * grad_raw) + jnp.sum(bias_raw * bias_raw)
    total_squares = lax.psum(local_squares, ("grp", "lat"))
    entries = (weight.shape[0] + 1) * weight.shape[1] * lax.axis_size("lat") * lax.axis_size("grp")
    factor = jnp.minimum(1.0, 1.0 / jnp.sqrt(total_squares / entries + epsilon))
    return (
        (grad_raw * factor).astype(jnp.bfloat16),
        bias_raw * factor,
        error_own.astype(jnp.bfloat16),
    )


def solution(mesh):
    return jax.shard_map(
        body,
        mesh=mesh,
        in_specs=(P("lat", None), P(), P(None, ("grp", "lat")), P(("grp", "lat")), P()),
        out_specs=(P(None, ("grp", "lat")), P(("grp", "lat")), P("lat", None)),
        check_vma=False,
    )
```

profile of v0, /device:TPU:1, one launch (start us, length us, event | category | flops | bytes accessed | tf_op | source)
XLA Modules:
  0.0 528.7 jit_solution(4097323418237096294)
XLA Ops:
  7.2 0.7 all-gather.3.cloned.1.call-update
  7.9 0.0 reduce-scatter.2.cloned.1.call-start
  8.0 0.7 compare_select_fusion.1
  8.7 0.7 compare_and_fusion
  9.3 68.9 %all-gather.3.cloned.1.call-done = bf16[256,8192]{1,0:T(8,128)(2,1)} async-done(((bf16[8,8192]{1,0:T(8,128)(2,1)}), bf16[256,8192]{1,0:T(8,128)(2,1)}) %all-gather.3.cloned.1.call-update) | async-done | bytes 4194320 | tf_op jit(solution)/shard_map/all_gather | solution.py:14
  78.3 11.7 %gather_fusion = bf16[256,8192]{1,0:T(8,128)(2,1)} fusion(bf16[256,8192]{1,0:T(8,128)(2,1)} %all-gather.3.cloned.1.call-done, s32[1024]{0:T(1024)S(1)} %pad_clamp_fusion), kind=kCustom, calls=%fused_computation | custom fusion | bytes 8389632 | tf_op jit(solution)/shard_map/jit(_take)/gather | solution.py:15
  90.0 2.7 broadcast_select_fusion
  92.7 1.9 copy-done.1
  94.6 1.3 fusion.4
  95.9 3.2 convolution_convert_fusion
  99.2 0.0 all-reduce.2.cloned.1.call-start
  99.2 102.6 %reduce-scatter.2.cloned.1.call-done = bf16[8,8192]{1,0:T(8,128)(2,1)} async-done(((bf16[256,8192]{1,0:T(8,128)(2,1)}), bf16[8,8192]{1,0:T(8,128)(2,1)}) %reduce-scatter.2.cloned.1.call-update) | async-done | bytes 131088 | tf_op jit(solution)/shard_map/reduce_scatter | solution.py:21
  201.8 0.2 all-gather.5.cloned.1.call-start
  202.0 128.7 %all-reduce.2.cloned.1.call-done = bf16[8,8192]{1,0:T(8,128)(2,1)} async-done(((bf16[8,8192]{1,0:T(8,128)(2,1)}), bf16[8,8192]{1,0:T(8,128)(2,1)}) %all-reduce.2.cloned.1.call-update) | async-done | bytes 131088 | tf_op jit(solution)/shard_map/psum | solution.py:29
  330.7 1.7 fusion.5
  332.5 69.7 %all-gather.5.cloned.1.call-done = bf16[256,8192]{1,0:T(8,128)(2,1)} async-done(((bf16[8,8192]{1,0:T(8,128)(2,1)}), bf16[256,8192]{1,0:T(8,128)(2,1)}) %all-gather.5.cloned.1.call-update) | async-done | bytes 4194320 | tf_op jit(solution)/shard_map/all_gather | solution.py:32
  402.2 3.6 fusion.11
  405.8 1.5 fusion
  407.3 0.6 multiply_reduce_fusion.1
  407.9 0.1 copy-done.3
  408.0 4.4 multiply_reduce_fusion
  413.6 103.6 %psum.15 = f32[]{:T(128)} all-reduce(f32[]{:T(128)S(6)} %add.67), channel_id=1, replica_groups=mesh['grp'=16,'lat'=32] {'grp','lat'}, use_global_device_ids=true, to_apply=%region_5.6 | all-reduce | flops 1 | bytes 8 | tf_op jit(solution)/shard_map/psum | solution.py:47
  518.0 0.5 broadcast_multiply_fusion
  518.5 3.7 multiply_convert_fusion
  (15 shorter events, 0.1 us)
Async XLA Ops:
  7.2 87.4 %copy-start = (bf16[8192,128]{1,0:T(8,128)(2,1)S(1)}, bf16[8192,128]{1,0:T(8,128)(2,1)}, u32[]{:S(2)}) copy-start(bf16[8192,128]{1,0:T(8,128)(2,1)} %param.7) | copy-start | bytes 6291460
  7.2 71.1 %all-gather.3.cloned.1.call-start = ((), (), s32[]{:S(2)}) async-start(), calls=%async_computation.1 | async-start | bytes 4325376 | tf_op jit(solution)/shard_map/all_gather | solution.py:14
  7.9 193.9 %reduce-scatter.2.cloned.1.call-start = ((), (), s32[]{:S(2)}) async-start(), calls=%async_computation.2 | async-start | bytes 4325376 | tf_op jit(solution)/shard_map/reduce_scatter | solution.py:21
  90.0 4.6 copy-start.4
  90.0 4.6 copy-start.5
  92.6 1.9 copy-start.1
  99.2 231.6 %all-reduce.2.cloned.1.call-start = ((), (), s32[]{:S(2)}) async-start(), calls=%async_computation.3 | async-start | bytes 262144 | tf_op jit(solution)/shard_map/psum | solution.py:29
  201.8 200.4 %all-gather.5.cloned.1.call-start = ((), (), s32[]{:S(2)}) async-start(), calls=%async_computation.4 | async-start | bytes 4325376 | tf_op jit(solution)/shard_map/all_gather | solution.py:32
  402.2 3.6 copy-start.2
  405.8 2.2 copy-start.3
Sparse Core Ops, SparseCore 0:
  11.1 67.0 all-gather.2
  99.3 102.4 reduce-scatter.1
  204.2 126.4 all-reduce.1
  334.3 67.8 all-gather.4
where the time goes:
time: 529 us
  waiting for transfers between devices  371 us (70%)
  blocking collectives  104 us (20%)
  between operations  15.8 us (3%)
  matrix products  14 us (3%)
  local copies, waits for them, and re-layouts  13.7 us (3%)
  other arithmetic  10.6 us (2%)
    psum x1, waiting for transfers between devices, body(): recon = lax.psum(block_recon, 'grp').astype(jnp.float32)  129 us
    psum x1, blocking collectives, body(): total_squares = lax.psum(local_squares, ('grp', 'lat'))  104 us
    reduce_scatter x1, waiting for transfers between devices, body(): lax.psum_scatter(lax.dot_general(active, weight, (((1,), (1,)), ((), ()))...  103 us
    all_gather x1, waiting for transfers between devices, body(): grad_rows = lax.all_gather(grad_own, 'lat', axis=0, tiled=True)  69.7 us
    all_gather x1, waiting for transfers between devices, body(): gathered = lax.all_gather(stream, 'lat', axis=0, tiled=True)  68.9 us
    gather x1, local copies, waits for them, and re-layouts, body(): batch = jnp.take(gathered, batch_index, axis=0)  11.7 us
  transfers between devices with their start and end apart: 4, of which 4 were waited for; matrix products, arithmetic and copies ran while one was open for 0% of the time, Pallas kernels for 0%

commit v1 on v0

--- a/solution.py
+++ b/solution.py
@@ -26,7 +26,7 @@
         scatter_dimension=0,
         tiled=True,
     )
-    recon = lax.psum(block_recon, "grp").astype(jnp.float32)
+    recon = jnp.sum(lax.all_gather(block_recon, "grp"), axis=0).astype(jnp.float32)
     error_own = recon + dec_bias - own_batch.astype(jnp.float32)
     grad_own = (2.0 * error_own).astype(jnp.bfloat16)
     grad_rows = lax.all_gather(grad_own, "lat", axis=0, tiled=True)

time: 529 us -> 468 us (0.88)
  waiting for transfers between devices: 371 us -> 308 us
    psum x1 -> x0, waiting for transfers between devices: 129 us -> none  [body(): recon = lax.psum(block_recon, 'grp').astype(jnp.float32)]
    all_gather x0 -> x1, waiting for transfers between devices: none -> 67.2 us  [body(): lax.all_gather(block_recon, 'grp')]
where the time goes in v1:
time: 468 us
  waiting for transfers between devices  308 us (66%)
  blocking collectives  104 us (22%)
  between operations  15.8 us (3%)
  matrix products  14 us (3%)
  local copies, waits for them, and re-layouts  13.7 us (3%)
  other arithmetic  12.4 us (3%)
    psum x1, blocking collectives, body(): total_squares = lax.psum(local_squares, ('grp', 'lat'))  104 us
    reduce_scatter x1, waiting for transfers between devices, body(): lax.psum_scatter(lax.dot_general(active, weight, (((1,), (1,)), ((), ()))...  103 us
    all_gather x1, waiting for transfers between devices, body(): gathered = lax.all_gather(stream, 'lat', axis=0, tiled=True)  68.9 us
    all_gather x1, waiting for transfers between devices, body(): grad_rows = lax.all_gather(grad_own, 'lat', axis=0, tiled=True)  68.3 us
    all_gather x1, waiting for transfers between devices, body(): lax.all_gather(block_recon, 'grp')  67.2 us
    gather x1, local copies, waits for them, and re-layouts, body(): batch = jnp.take(gathered, batch_index, axis=0)  11.7 us
  transfers between devices with their start and end apart: 4, of which 4 were waited for; matrix products, arithmetic and copies ran while one was open for 0% of the time, Pallas kernels for 0%

profile of v1, /device:TPU:1, one launch (start us, length us, event | category | flops | bytes accessed | tf_op | source)
XLA Modules:
  0.0 467.7 jit_solution(14080454699518466450)
XLA Ops:
  7.2 0.7 all-gather.5.cloned.1.call-update
  8.0 0.7 compare_select_fusion.1
  8.7 0.7 compare_and_fusion
  9.3 68.9 %all-gather.5.cloned.1.call-done = bf16[256,8192]{1,0:T(8,128)(2,1)} async-done(((bf16[8,8192]{1,0:T(8,128)(2,1)}), bf16[256,8192]{1,0:T(8,128)(2,1)}) %all-gather.5.cloned.1.call-update) | async-done | bytes 4194320 | tf_op jit(solution)/shard_map/all_gather | solution.py:14
  78.3 11.7 %gather_fusion = bf16[256,8192]{1,0:T(8,128)(2,1)} fusion(bf16[256,8192]{1,0:T(8,128)(2,1)} %all-gather.5.cloned.1.call-done, s32[1024]{0:T(1024)S(1)} %pad_clamp_fusion), kind=kCustom, calls=%fused_computation | custom fusion | bytes 8389632 | tf_op jit(solution)/shard_map/jit(_take)/gather | solution.py:15
  90.0 2.7 broadcast_select_fusion
  92.7 1.9 copy-done.1
  94.6 1.3 fusion.4
  95.9 3.2 convolution_convert_fusion
  99.2 0.0 all-gather.9.cloned.1.call-start
  99.2 102.6 %reduce-scatter.2.cloned.1.call-done = bf16[8,8192]{1,0:T(8,128)(2,1)} async-done(((bf16[256,8192]{1,0:T(8,128)(2,1)}), bf16[8,8192]{1,0:T(8,128)(2,1)}) %reduce-scatter.2.cloned.1.call-update) | async-done | bytes 131088 | tf_op jit(solution)/shard_map/reduce_scatter | solution.py:21
  201.8 0.2 all-gather.7.cloned.1.call-start
  202.0 67.2 %all-gather.9.cloned.1.call-done = bf16[128,8192]{1,0:T(8,128)(2,1)} async-done(((bf16[8,8192]{1,0:T(8,128)(2,1)}), bf16[128,8192]{1,0:T(8,128)(2,1)}) %all-gather.9.cloned.1.call-update) | async-done | bytes 2097168 | tf_op jit(solution)/shard_map/all_gather | solution.py:29
  269.3 1.9 bitcast_reduce_fusion
  271.1 1.7 fusion.5
  272.8 68.3 %all-gather.7.cloned.1.call-done = bf16[256,8192]{1,0:T(8,128)(2,1)} async-done(((bf16[8,8192]{1,0:T(8,128)(2,1)}), bf16[256,8192]{1,0:T(8,128)(2,1)}) %all-gather.7.cloned.1.call-update) | async-done | bytes 4194320 | tf_op jit(solution)/shard_map/all_gather | solution.py:32
  341.2 3.6 fusion.11
  344.8 1.5 fusion
  346.3 0.6 multiply_reduce_fusion.1
  346.9 0.1 copy-done.3
  347.0 4.4 multiply_reduce_fusion
  352.6 103.6 %psum.7 = f32[]{:T(128)} all-reduce(f32[]{:T(128)S(6)} %add.65), channel_id=1, replica_groups=mesh['grp'=16,'lat'=32] {'grp','lat'}, use_global_device_ids=true, to_apply=%region_5.6 | all-reduce | flops 1 | bytes 8 | tf_op jit(solution)/shard_map/psum | solution.py:47
  456.9 0.5 broadcast_multiply_fusion
  457.5 3.7 multiply_convert_fusion
  (16 shorter events, 0.2 us)
Async XLA Ops:
  7.2 87.4 %copy-start = (bf16[8192,128]{1,0:T(8,128)(2,1)S(1)}, bf16[8192,128]{1,0:T(8,128)(2,1)}, u32[]{:S(2)}) copy-start(bf16[8192,128]{1,0:T(8,128)(2,1)} %param.7) | copy-start | bytes 6291460
  7.2 71.1 %all-gather.5.cloned.1.call-start = ((), (), s32[]{:S(2)}) async-start(), calls=%async_computation.1 | async-start | bytes 4325376 | tf_op jit(solution)/shard_map/all_gather | solution.py:14
  7.9 193.9 %reduce-scatter.2.cloned.1.call-start = ((), (), s32[]{:S(2)}) async-start(), calls=%async_computation.2 | async-start | bytes 4325376 | tf_op jit(solution)/shard_map/reduce_scatter | solution.py:21
  90.0 4.6 copy-start.4
  90.0 4.6 copy-start.5
  92.6 1.9 copy-start.1
  99.2 170.1 %all-gather.9.cloned.1.call-start = ((), (), s32[]{:S(2)}) async-start(), calls=%async_computation.4 | async-start | bytes 2228224 | tf_op jit(solution)/shard_map/all_gather | solution.py:29
  201.8 139.4 %all-gather.7.cloned.1.call-start = ((), (), s32[]{:S(2)}) async-start(), calls=%async_computation.3 | async-start | bytes 4325376 | tf_op jit(solution)/shard_map/all_gather | solution.py:32
  341.2 3.6 copy-start.2
  344.8 2.2 copy-start.3
Sparse Core Ops, SparseCore 0:
  11.1 67.0 all-gather.4
  99.3 102.4 reduce-scatter.1
  204.1 65.1 all-gather.8
  273.3 67.8 all-gather.6
